TPU v7x, 32 devices: a whole 2x2x4 slice. The times are simulated.
32 devices in a mesh: var: 8 (over z, y), samp: 4 (over x, core).
Axes of the slice: x: 2, y: 2, z: 4, core: 2. Of those that a mesh axis runs over, the one named last changes fastest.
Arguments:
- dosages: bfloat16 [8192, 6144], P('samp', 'var'), may hold values from 0 to 2
- observed: int32 [8192, 6144], P('samp', 'var'), may hold values 0 or 1
Outputs:
- ld_scores: float32 [6144], P(('var', 'samp'))
All inputs are finite; a program needn't handle non-finite values. No bound on the sum of `observed` on one device may be relied on, other than what follows from the above.
Results may differ from a plain program's by a relative error of at most 0.00055.
Values may be sent and summed in bfloat16 or wider, within the bound.
No kernel may reach another device: no remote copies, remote signals or barrier semaphores. Data moves between devices by JAX's collectives and lax.ppermute only.
A program may use at most 192 MiB of HBM per device.

v0:
```python
import jax
import jax.numpy as jnp
from jax import lax
from jax.sharding import PartitionSpec as P

BAND = 3
PARTNER_STEP = {1: 1, 2: 2, 3: -3}
PROCESS_ORDER = (2, 3, 1)


def from_behind(value, axis, steps):
    count = lax.axis_size(axis)
    leading, last = (max(0, -steps), min(count, count - steps))
    return lax.ppermute(value, axis, [(source, source + steps) for source in range(leading, last)])


def adjusted_r2(gram_part, samples):
    correl = gram_part / samples
    squared = correl * correl
    return squared - (1.0 - squared) / (samples - 2)


def gram_of(left, right):
    return lax.dot_general(
        left, right, (((0,), (0,)), ((), ())), preferred_element_type=jnp.float32
    )


def reduce_to_owner(part, owner, n_samp):
    pairs_core = [(s, s ^ 1) for s in range(n_samp) if s & 1 != owner & 1]
    summed = part + lax.ppermute(part.astype(jnp.bfloat16), "samp", pairs_core).astype(jnp.float32)
    pairs_chip = [(owner ^ 2, owner)]
    return summed + lax.ppermute(summed.astype(jnp.bfloat16), "samp", pairs_chip).astype(
        jnp.float32
    )


def local(dosages, observed):
    coded = jnp.where(observed != 0, dosages, jnp.asarray(-1, dosages.dtype))
    raw = {
        offset: from_behind(coded, "var", -PARTNER_STEP[offset]) for offset in range(1, BAND + 1)
    }
    values = dosages.astype(jnp.float32)
    present = observed.astype(jnp.float32)
    n_samp = lax.axis_size("samp")
    n_var = lax.axis_size("var")
    position = lax.axis_index("var")
    me = lax.axis_index("samp")
    partial = jnp.stack(
        [jnp.sum(present, 0), jnp.sum(present * values, 0), jnp.sum(present * values * values, 0)]
    )
    slots = jnp.zeros((n_var,) + partial.shape, jnp.float32)
    stats = lax.psum(lax.dynamic_update_index_in_dim(slots, partial, position, 0), ("var", "samp"))
    seen_count = jnp.maximum(stats[:, 0], 1.0)
    column_mean = stats[:, 1] / seen_count
    spread = stats[:, 2] / seen_count - column_mean * column_mean
    inverse_sd = lax.rsqrt(spread + 1e-05)
    own_mean = lax.dynamic_index_in_dim(column_mean, position, 0, keepdims=False)
    own_sd = lax.dynamic_index_in_dim(inverse_sd, position, 0, keepdims=False)
    standard = ((values - own_mean) * own_sd * present).astype(jnp.bfloat16)
    samples = standard.shape[0] * n_samp
    block_width = standard.shape[1]
    owned = {0: reduce_to_owner(gram_of(standard, standard), 0, n_samp)}
    arrived, owned[0] = lax.optimization_barrier(([raw[d] for d in PROCESS_ORDER], owned[0]))
    for offset, coded_partner in zip(PROCESS_ORDER, arrived):
        source = jnp.clip(position + PARTNER_STEP[offset], 0, n_var - 1)
        partner_mean = lax.dynamic_index_in_dim(column_mean, source, 0, keepdims=False)
        partner_sd = lax.dynamic_index_in_dim(inverse_sd, source, 0, keepdims=False)
        partner_values = coded_partner.astype(jnp.float32)
        partner_present = (partner_values >= 0).astype(jnp.float32)
        partner = ((partner_values - partner_mean) * partner_sd * partner_present).astype(
            jnp.bfloat16
        )
        owned[offset] = reduce_to_owner(gram_of(standard, partner), offset, n_samp)
    gram = lax.dynamic_index_in_dim(
        jnp.stack([owned[d] for d in range(BAND + 1)]), me, 0, keepdims=False
    )
    steps = jnp.array([0] + [PARTNER_STEP[d] for d in range(1, BAND + 1)], jnp.int32)
    target = position + steps[me]
    in_range = ((target >= 0) & (target < n_var)).astype(jnp.float32)
    adjusted = adjusted_r2(gram, samples) * in_range
    row_sums = jnp.sum(adjusted, 1)
    col_sums = jnp.sum(adjusted, 0) * (me > 0).astype(jnp.float32)
    pairs = []
    for var_idx in range(n_var):
        for offset in range(1, BAND + 1):
            dest = var_idx + PARTNER_STEP[offset]
            if 0 <= dest < n_var:
                pairs.append((var_idx * n_samp + offset, dest * n_samp + offset))
    moved = lax.ppermute(col_sums, ("var", "samp"), pairs)
    total = lax.psum_scatter(row_sums + moved, "samp", scatter_dimension=0, tiled=True)
    return total / block_width


def solution(mesh):
    placed = (P("samp", "var"), P("samp", "var"))
    return jax.shard_map(
        local, mesh=mesh, in_specs=placed, out_specs=P(("var", "samp")), check_vma=False
    )
```

profile of v0, /device:TPU:0, one launch (start us, length us, event | category | flops | bytes accessed | tf_op | source)
XLA Modules:
  0.0 372.2 jit_solution(16671350342384689641)
XLA Ops:
  6.5 0.0 all-reduce.3.cloned.1.call-start
  6.5 5.4 %fusion.13 = (f32[768]{0:T(1024)S(1)}, f32[768]{0:T(1024)S(1)}, f32[768]{0:T(1024)S(1)}) fusion(bf16[2048,768]{1,0:T(8,128)(2,1)} %param.3, s32[2048,768]{1,0:T(8,128)} %param.4), kind=kLoop, calls=%fused_computation.28 | loop fusion | flops 11007744 | bytes 9446400 | tf_op jit(solution)/shard_map/reduce_sum | solution.py:50
  12.0 0.0 copy-start.10
  12.1 0.6 copy-done.10
  12.7 0.0 all-reduce.3.cloned.1.call-update
  12.7 0.0 copy-done
  12.7 5.3 %compare_select_fusion = bf16[2048,768]{1,0:T(8,128)(2,1)} fusion(bf16[2048,768]{1,0:T(8,128)(2,1)S(1)} %copy-done, s32[2048,768]{1,0:T(8,128)} %param.4), kind=kLoop, calls=%fused_computation.27 | loop fusion | flops 3145728 | bytes 12582912 | tf_op jit(solution)/shard_map/jit(_where)/select_n | solution.py:39
  18.0 1.3 collective-permute-start
  19.3 8.7 %collective-permute-start.1 = (bf16[2048,768]{1,0:T(8,128)(2,1)}, bf16[2048,768]{1,0:T(8,128)(2,1)}, u32[]{:S(2)}, u32[]{:S(2)}) collective-permute-start(bf16[2048,768]{1,0:T(8,128)(2,1)} %compare_select_fusion), channel_id=1, source_target_pairs={{0,12},{4,16},{8,20},{12,24},{16,28},{1,13},{5,17},{9,21},{13,25},... | collective-permute-start | bytes 9437192 | tf_op jit(solution)/shard_map/ppermute | solution.py:14
  27.9 1.3 collective-permute-start.2
  29.2 232.4 %all-reduce.3.cloned.1.call-done = f32[8,3,768]{2,1,0:T(4,128)} async-done(((f32[8,3,768]{2,1,0:T(4,128)}), f32[8,3,768]{2,1,0:T(4,128)}) %all-reduce.3.cloned.1.call-update) | async-done | bytes 73744 | tf_op jit(solution)/shard_map/psum | solution.py:53
  261.6 1.1 add_rsqrt_fusion
  262.7 0.1 fusion.43
  262.8 3.9 %fusion.12 = bf16[2048,768]{1,0:T(8,128)(2,1)S(1)} fusion(bf16[2048,768]{1,0:T(8,128)(2,1)S(1)} %copy-done, s32[2048,768]{1,0:T(8,128)} %param.4, f32[768]{0:T(1024)S(1)} %get-tuple-element.37, f32[768]{0:T(1024)S(1)} %get-tuple-element.21), kind=kLoop, calls=%fused_computation.25 | loop fusion | flops 9437184 | bytes 12589056 | tf_op jit(solution)/shard_map/convert_element_type | solution.py:60
  266.8 2.7 fusion.53
  269.5 1.3 collective-permute-start.3
  270.8 3.4 collective-permute-done.3
  274.2 0.3 fusion.35
  274.5 1.3 collective-permute-start.4
  275.8 16.8 %collective-permute-done.4 = bf16[768,768]{1,0:T(8,128)(2,1)S(1)} collective-permute-done((bf16[768,768]{1,0:T(8,128)(2,1)S(1)}, bf16[768,768]{1,0:T(8,128)(2,1)S(1)}, u32[]{:S(2)}, u32[]{:S(2)}) %collective-permute-start.4) | collective-permute-done | bytes 1179680 | tf_op jit(solution)/shard_map/ppermute | solution.py:33
  292.6 1.7 convert_add_fusion.3
  294.3 0.0 collective-permute-done
  294.3 0.0 collective-permute-done.1
  294.3 0.0 collective-permute-done.2
  294.3 4.8 %fusion.56 = (bf16[768,768]{1,0:T(8,128)(2,1)S(1)}, f32[768,768]{1,0:T(8,128)S(1)}) fusion(bf16[2048,768]{1,0:T(8,128)(2,1)S(1)} %fusion.12, bf16[2048,768]{1,0:T(8,128)(2,1)} %collective-permute-done.2, f32[768]{0:T(1024)S(1)} %get-tuple-element.39, f32[768]{0:T(1024)S(1)} %get-tuple-element.18), kind=kOutput, calls=%fused_computation.92 | convolution fusion | flops 2425946112 | bytes 9836544 | tf_op jit(solution)/shard_map/dot_general | solution.py:24
  299.1 1.5 collective-permute-start.5
  300.7 4.8 %fusion.55 = (bf16[768,768]{1,0:T(8,128)(2,1)S(1)}, f32[768,768]{1,0:T(8,128)S(1)}) fusion(bf16[2048,768]{1,0:T(8,128)(2,1)S(1)} %fusion.12, bf16[2048,768]{1,0:T(8,128)(2,1)} %collective-permute-done, f32[768]{0:T(1024)S(1)} %get-tuple-element.38, f32[768]{0:T(1024)S(1)} %get-tuple-element.20), kind=kOutput, calls=%fused_computation.91 | convolution fusion | flops 2425946112 | bytes 9836544 | tf_op jit(solution)/shard_map/dot_general | solution.py:24
  305.5 0.0 copy-start.1
  305.5 1.3 collective-permute-start.7
  306.8 4.8 %fusion.54 = (bf16[768,768]{1,0:T(8,128)(2,1)S(1)}, f32[768,768]{1,0:T(8,128)S(1)}) fusion(bf16[2048,768]{1,0:T(8,128)(2,1)S(1)} %fusion.12, bf16[2048,768]{1,0:T(8,128)(2,1)} %collective-permute-done.1, f32[768]{0:T(1024)S(1)} %get-tuple-element.36, f32[768]{0:T(1024)S(1)} %get-tuple-element.19), kind=kOutput, calls=%fused_computation.90 | convolution fusion | flops 2425946112 | bytes 9836544 | tf_op jit(solution)/shard_map/dot_general | solution.py:24
  311.7 0.0 copy-start.3
  311.7 3.2 collective-permute-start.9
  314.8 0.0 collective-permute-done.5
  314.8 1.3 fusion.36
  316.1 1.7 collective-permute-start.6
  317.8 0.0 collective-permute-done.7
  317.8 0.0 copy-done.1
  317.8 1.4 fusion.37
  319.2 0.0 copy-done.6
  319.3 2.5 collective-permute-start.8
  321.7 0.0 collective-permute-done.9
  321.7 0.0 copy-done.3
  321.8 1.5 fusion.38
  323.2 0.0 copy-done.8
  323.2 1.8 collective-permute-start.10
  325.0 0.0 copy-done.12
  325.0 0.6 dynamic_slice.41
  326.2 0.0 copy-start.2
  326.3 0.0 collective-permute-done.6
  326.3 1.7 add_bitcast_fusion.2
  328.0 14.3 %collective-permute-done.8 = bf16[768,768]{1,0:T(8,128)(2,1)} collective-permute-done((bf16[768,768]{1,0:T(8,128)(2,1)}, bf16[768,768]{1,0:T(8,128)(2,1)}, u32[]{:S(2)}, u32[]{:S(2)}) %collective-permute-start.8) | collective-permute-done | bytes 1179680 | tf_op jit(solution)/shard_map/ppermute | solution.py:33
  342.4 0.0 copy-done.7
  342.4 1.7 add_bitcast_fusion.1
  344.1 0.0 collective-permute-done.10
  344.1 0.0 copy-done.4
  344.1 0.0 copy-done.9
  344.1 1.8 add_bitcast_fusion
  345.9 0.2 copy-done.5
  346.1 1.2 fusion.52
  347.3 0.7 collective-permute-start.11
  348.0 0.6 dynamic-slice.8
  349.2 0.0 collective-permute-done.11
  349.2 15.5 %all-reduce = f32[768]{0:T(1024)S(1)} all-reduce(f32[768]{0:T(1024)S(1)} %add.83), channel_id=2, replica_groups=mesh['var'=8,'samp'=4] {'samp'}, use_global_device_ids=true, to_apply=%region_6.7.clone | all-reduce | flops 768 | bytes 6144
  364.7 0.6 dynamic-slice_multiply_fusion
  (18 shorter events, 0.1 us)
Async XLA Ops:
  6.5 255.1 %all-reduce.3.cloned.1.call-start = ((), (), s32[]{:S(2)}) async-start(), calls=%async_computation | async-start | bytes 196608 | tf_op jit(solution)/shard_map/psum | solution.py:53
  6.5 6.2 %copy-start = (bf16[2048,768]{1,0:T(8,128)(2,1)S(1)}, bf16[2048,768]{1,0:T(8,128)(2,1)}, u32[]{:S(2)}) copy-start(bf16[2048,768]{1,0:T(8,128)(2,1)} %param.3) | copy-start | bytes 9437188
  12.0 0.6 copy-start.10
  18.0 276.4 %collective-permute-start = (bf16[2048,768]{1,0:T(8,128)(2,1)}, bf16[2048,768]{1,0:T(8,128)(2,1)}, u32[]{:S(2)}, u32[]{:S(2)}) collective-permute-start(bf16[2048,768]{1,0:T(8,128)(2,1)} %compare_select_fusion), channel_id=1, source_target_pairs={{8,0},{12,4},{16,8},{20,12},{24,16},{28,20},{9,1},{13,5},{17,9},{2... | collective-permute-start | bytes 9437192 | tf_op jit(solution)/shard_map/ppermute | solution.py:14
  19.3 275.1 %collective-permute-start.1 = (bf16[2048,768]{1,0:T(8,128)(2,1)}, bf16[2048,768]{1,0:T(8,128)(2,1)}, u32[]{:S(2)}, u32[]{:S(2)}) collective-permute-start(bf16[2048,768]{1,0:T(8,128)(2,1)} %compare_select_fusion), channel_id=1, source_target_pairs={{0,12},{4,16},{8,20},{12,24},{16,28},{1,13},{5,17},{9,21},{13,25},... | collective-permute-start | bytes 9437192 | tf_op jit(solution)/shard_map/ppermute | solution.py:14
  27.9 266.4 %collective-permute-start.2 = (bf16[2048,768]{1,0:T(8,128)(2,1)}, bf16[2048,768]{1,0:T(8,128)(2,1)}, u32[]{:S(2)}, u32[]{:S(2)}) collective-permute-start(bf16[2048,768]{1,0:T(8,128)(2,1)} %compare_select_fusion), channel_id=1, source_target_pairs={{4,0},{8,4},{12,8},{16,12},{20,16},{24,20},{28,24},{5,1},{9,5},{13... | collective-permute-start | bytes 9437192 | tf_op jit(solution)/shard_map/ppermute | solution.py:14
  269.5 4.7 %collective-permute-start.3 = (bf16[768,768]{1,0:T(8,128)(2,1)S(1)}, bf16[768,768]{1,0:T(8,128)(2,1)S(1)}, u32[]{:S(2)}, u32[]{:S(2)}) collective-permute-start(bf16[768,768]{1,0:T(8,128)(2,1)S(1)} %get-tuple-element.28), channel_id=1, source_target_pairs={{1,0},{3,2},{5,4},{7,6},{9,8},{11,10},{13,12},{15,14},{17,16},{19,... | collective-permute-start | bytes 3538952 | tf_op jit(solution)/shard_map/ppermute | solution.py:31
  274.5 18.1 %collective-permute-start.4 = (bf16[768,768]{1,0:T(8,128)(2,1)S(1)}, bf16[768,768]{1,0:T(8,128)(2,1)S(1)}, u32[]{:S(2)}, u32[]{:S(2)}) collective-permute-start(bf16[768,768]{1,0:T(8,128)(2,1)S(1)} %fusion.35), channel_id=1, source_target_pairs={{2,0},{6,4},{10,8},{14,12},{18,16},{22,20},{26,24},{30,28}} | collective-permute-start | bytes 3538952 | tf_op jit(solution)/shard_map/ppermute | solution.py:33
  299.1 15.7 %collective-permute-start.5 = (bf16[768,768]{1,0:T(8,128)(2,1)S(1)}, bf16[768,768]{1,0:T(8,128)(2,1)S(1)}, u32[]{:S(2)}, u32[]{:S(2)}) collective-permute-start(bf16[768,768]{1,0:T(8,128)(2,1)S(1)} %get-tuple-element.34), channel_id=1, source_target_pairs={{0,1},{2,3},{4,5},{6,7},{8,9},{10,11},{12,13},{14,15},{16,17},{18,... | collective-permute-start | bytes 3538952 | tf_op jit(solution)/shard_map/ppermute | solution.py:31
  305.5 12.3 %copy-start.1 = (f32[768,768]{1,0:T(8,128)}, f32[768,768]{1,0:T(8,128)S(1)}, u32[]{:S(2)}) copy-start(f32[768,768]{1,0:T(8,128)S(1)} %get-tuple-element.33) | copy-start | bytes 7077892
  305.5 12.3 %collective-permute-start.7 = (bf16[768,768]{1,0:T(8,128)(2,1)S(1)}, bf16[768,768]{1,0:T(8,128)(2,1)S(1)}, u32[]{:S(2)}, u32[]{:S(2)}) collective-permute-start(bf16[768,768]{1,0:T(8,128)(2,1)S(1)} %get-tuple-element.32), channel_id=1, source_target_pairs={{1,0},{3,2},{5,4},{7,6},{9,8},{11,10},{13,12},{15,14},{17,16},{19,... | collective-permute-start | bytes 3538952 | tf_op jit(solution)/shard_map/ppermute | solution.py:31
  311.7 10.1 %copy-start.3 = (f32[768,768]{1,0:T(8,128)}, f32[768,768]{1,0:T(8,128)S(1)}, u32[]{:S(2)}) copy-start(f32[768,768]{1,0:T(8,128)S(1)} %get-tuple-element.31) | copy-start | bytes 7077892
  311.7 10.1 %collective-permute-start.9 = (bf16[768,768]{1,0:T(8,128)(2,1)S(1)}, bf16[768,768]{1,0:T(8,128)(2,1)S(1)}, u32[]{:S(2)}, u32[]{:S(2)}) collective-permute-start(bf16[768,768]{1,0:T(8,128)(2,1)S(1)} %get-tuple-element.30), channel_id=1, source_target_pairs={{0,1},{2,3},{4,5},{6,7},{8,9},{10,11},{12,13},{14,15},{16,17},{18,... | collective-permute-start | bytes 3538952 | tf_op jit(solution)/shard_map/ppermute | solution.py:31
  316.1 10.1 %collective-permute-start.6 = (bf16[768,768]{1,0:T(8,128)(2,1)}, bf16[768,768]{1,0:T(8,128)(2,1)}, u32[]{:S(2)}, u32[]{:S(2)}) collective-permute-start(bf16[768,768]{1,0:T(8,128)(2,1)} %fusion.36), channel_id=1, source_target_pairs={{3,1},{7,5},{11,9},{15,13},{19,17},{23,21},{27,25},{31,29}} | collective-permute-start | bytes 3538952 | tf_op jit(solution)/shard_map/ppermute | solution.py:33
  317.8 1.4 copy-start.6
  319.3 23.1 %collective-permute-start.8 = (bf16[768,768]{1,0:T(8,128)(2,1)}, bf16[768,768]{1,0:T(8,128)(2,1)}, u32[]{:S(2)}, u32[]{:S(2)}) collective-permute-start(bf16[768,768]{1,0:T(8,128)(2,1)} %fusion.37), channel_id=1, source_target_pairs={{0,2},{4,6},{8,10},{12,14},{16,18},{20,22},{24,26},{28,30}} | collective-permute-start | bytes 3538952 | tf_op jit(solution)/shard_map/ppermute | solution.py:33
  321.7 1.5 copy-start.8
  321.7 3.3 copy-start.12
  323.2 20.8 %collective-permute-start.10 = (bf16[768,768]{1,0:T(8,128)(2,1)}, bf16[768,768]{1,0:T(8,128)(2,1)}, u32[]{:S(2)}, u32[]{:S(2)}) collective-permute-start(bf16[768,768]{1,0:T(8,128)(2,1)} %fusion.38), channel_id=1, source_target_pairs={{1,3},{5,7},{9,11},{13,15},{17,19},{21,23},{25,27},{29,31}} | collective-permute-start | bytes 3538952 | tf_op jit(solution)/shard_map/ppermute | solution.py:33
  326.2 16.1 %copy-start.2 = (f32[768,768]{1,0:T(8,128)S(1)}, f32[768,768]{1,0:T(8,128)}, u32[]{:S(2)}) copy-start(f32[768,768]{1,0:T(8,128)} %copy-done.1) | copy-start | bytes 7077892
  326.3 16.1 %copy-start.7 = (bf16[768,768]{1,0:T(8,128)(2,1)S(1)}, bf16[768,768]{1,0:T(8,128)(2,1)}, u32[]{:S(2)}) copy-start(bf16[768,768]{1,0:T(8,128)(2,1)} %copy-done.6) | copy-start | bytes 3538948
  328.0 16.0 %copy-start.4 = (f32[768,768]{1,0:T(8,128)S(1)}, f32[768,768]{1,0:T(8,128)}, u32[]{:S(2)}) copy-start(f32[768,768]{1,0:T(8,128)} %copy-done.3) | copy-start | bytes 7077892
  328.0 16.0 %copy-start.9 = (bf16[768,768]{1,0:T(8,128)(2,1)S(1)}, bf16[768,768]{1,0:T(8,128)(2,1)}, u32[]{:S(2)}) copy-start(bf16[768,768]{1,0:T(8,128)(2,1)} %copy-done.8) | copy-start | bytes 3538948
  344.0 2.0 copy-start.5
  346.1 1.9 copy-start.11
  347.3 1.9 collective-permute-start.11
Sparse Core Ops, SparseCore 0:
  12.9 248.6 all-reduce.2
where the time goes:
time: 373 us; the launch traced here: 372 us
  waiting for transfers between devices  267 us (72%)
  other arithmetic  29 us (8%)
  starting transfers between devices  26.4 us (7%)
  matrix products  17.2 us (5%)
  blocking collectives  15.5 us (4%)
  between operations  15 us (4%)
    psum x1, waiting for transfers between devices, local(): lax.psum(lax.dynamic_update_index_in_dim(slots, partial, position, 0), ('...  232 us
    ppermute x4, waiting for transfers between devices, reduce_to_owner(): lax.ppermute(summed.astype(jnp.bfloat16), 'samp', pairs_chip)  31.1 us
    dot_general x4, matrix products, gram_of(): lax.dot_general(left, right, (((0,), (0,)), ((), ())), preferred_element_...  17.2 us
    unnamed x1, blocking collectives  15.5 us
    ppermute x3, starting transfers between devices, from_behind(): lax.ppermute(value, axis, [(source, source + steps) for source in range(l...  11.2 us
  transfers between devices with their start and end apart: 13, of which 4 were waited for; matrix products, arithmetic and copies ran while one was open for 9% of the time, Pallas kernels for 0%

commit v1 on v0

--- a/solution.py
+++ b/solution.py
@@ -36,6 +36,12 @@
 
 
 def local(dosages, observed):
+
+    def _place_trails(piece_in):
+        odd = lax.all_gather(piece_in, ("var", "samp"))
+        passed = jnp.sum(odd, axis=0)
+        return passed
+
     coded = jnp.where(observed != 0, dosages, jnp.asarray(-1, dosages.dtype))
     raw = {
         offset: from_behind(coded, "var", -PARTNER_STEP[offset]) for offset in range(1, BAND + 1)
@@ -50,7 +56,7 @@
         [jnp.sum(present, 0), jnp.sum(present * values, 0), jnp.sum(present * values * values, 0)]
     )
     slots = jnp.zeros((n_var,) + partial.shape, jnp.float32)
-    stats = lax.psum(lax.dynamic_update_index_in_dim(slots, partial, position, 0), ("var", "samp"))
+    stats = _place_trails(lax.dynamic_update_index_in_dim(slots, partial, position, 0))
     seen_count = jnp.maximum(stats[:, 0], 1.0)
     column_mean = stats[:, 1] / seen_count
     spread = stats[:, 2] / seen_count - column_mean * column_mean

time: 373 us -> 299 us (0.80)
  waiting for transfers between devices: 267 us -> 194 us
    psum x1 -> x0, waiting for transfers between devices: 232 us -> none  [local(): lax.psum(lax.dynamic_update_index_in_dim(slots, partial, position, 0), ('...]
    all_gather x0 -> x1, waiting for transfers between devices: none -> 159 us  [_place_trails(): odd = lax.all_gather(piece_in, ('var', 'samp'))]
  transfers between devices with their start and end apart: 13 -> 13, of which waited for: 4 -> 4; matrix products, arithmetic and copies ran while one was open for 9% -> 11% of each run, Pallas kernels for 0% -> 0%
where the time goes in v1:
time: 299 us; the launch traced here: 298 us
  waiting for transfers between devices  194 us (65%)
  other arithmetic  29.7 us (10%)
  starting transfers between devices  26.4 us (9%)
  matrix products  17.1 us (6%)
  between operations  15.1 us (5%)
  blocking collectives  13.8 us (5%)
    all_gather x1, waiting for transfers between devices, _place_trails(): odd = lax.all_gather(piece_in, ('var', 'samp'))  159 us
    ppermute x4, waiting for transfers between devices, reduce_to_owner(): lax.ppermute(summed.astype(jnp.bfloat16), 'samp', pairs_chip)  31.1 us
    dot_general x4, matrix products, gram_of(): lax.dot_general(left, right, (((0,), (0,)), ((), ())), preferred_element_...  17.1 us
    unnamed x1, blocking collectives  13.8 us
    ppermute x3, starting transfers between devices, from_behind(): lax.ppermute(value, axis, [(source, source + steps) for source in range(l...  11.2 us
    ppermute x4, starting transfers between devices, reduce_to_owner(): lax.ppermute(part.astype(jnp.bfloat16), 'samp', pairs_core)  7.29 us
    ppermute x4, starting transfers between devices, reduce_to_owner(): lax.ppermute(summed.astype(jnp.bfloat16), 'samp', pairs_chip)  7.23 us
  transfers between devices with their start and end apart: 13, of which 4 were waited for; matrix products, arithmetic and copies ran while one was open for 11% of the time, Pallas kernels for 0%

profile of v1, /device:TPU:0, one launch (start us, length us, event | category | flops | bytes accessed | tf_op | source)
XLA Modules:
  0.0 298.3 jit_solution(7848624113319050425)
XLA Ops:
  6.5 0.0 all-gather.2.cloned.1.call-start
  6.5 5.4 %fusion.13 = (f32[768]{0:T(1024)S(1)}, f32[768]{0:T(1024)S(1)}, f32[768]{0:T(1024)S(1)}) fusion(bf16[2048,768]{1,0:T(8,128)(2,1)} %param.3, s32[2048,768]{1,0:T(8,128)} %param.4), kind=kLoop, calls=%fused_computation.28 | loop fusion | flops 11007744 | bytes 9446400 | tf_op jit(solution)/shard_map/reduce_sum | solution.py:56
  12.0 0.1 dynamic_update_slice.5
  12.2 0.0 copy-start.10
  12.2 0.6 copy-done.10
  12.8 0.0 all-gather.2.cloned.1.call-update
  12.8 0.0 copy-done
  12.8 5.3 %compare_select_fusion = bf16[2048,768]{1,0:T(8,128)(2,1)} fusion(bf16[2048,768]{1,0:T(8,128)(2,1)S(1)} %copy-done, s32[2048,768]{1,0:T(8,128)} %param.4), kind=kLoop, calls=%fused_computation.27 | loop fusion | flops 3145728 | bytes 12582912 | tf_op jit(solution)/shard_map/jit(_where)/select_n | solution.py:45
  18.1 1.3 collective-permute-start
  19.4 8.7 %collective-permute-start.1 = (bf16[2048,768]{1,0:T(8,128)(2,1)}, bf16[2048,768]{1,0:T(8,128)(2,1)}, u32[]{:S(2)}, u32[]{:S(2)}) collective-permute-start(bf16[2048,768]{1,0:T(8,128)(2,1)} %compare_select_fusion), channel_id=1, source_target_pairs={{0,12},{4,16},{8,20},{12,24},{16,28},{1,13},{5,17},{9,21},{13,25},... | collective-permute-start | bytes 9437192 | tf_op jit(solution)/shard_map/ppermute | solution.py:14
  28.1 1.3 collective-permute-start.2
  29.4 159.3 %all-gather.2.cloned.1.call-done = f32[32,8,3,768]{3,1,2,0:T(8,128)} async-done(((f32[1,8,3,768]{3,1,2,0:T(8,128)}), f32[32,8,3,768]{3,1,2,0:T(8,128)}) %all-gather.2.cloned.1.call-update) | async-done | bytes 2359312 | tf_op jit(solution)/shard_map/all_gather | solution.py:41
  188.7 1.8 reduce_sum.57
  190.5 0.1 dynamic-slice_reduce_fusion.2
  190.6 3.9 %fusion.12 = bf16[2048,768]{1,0:T(8,128)(2,1)S(1)} fusion(bf16[2048,768]{1,0:T(8,128)(2,1)S(1)} %copy-done, s32[2048,768]{1,0:T(8,128)} %param.4, f32[768]{0:T(1024)S(1)} %get-tuple-element.24, f32[768]{0:T(1024)S(1)} %get-tuple-element.36), kind=kLoop, calls=%fused_computation.25 | loop fusion | flops 9437184 | bytes 12589056 | tf_op jit(solution)/shard_map/convert_element_type | solution.py:66
  194.5 2.7 fusion.46
  197.2 1.3 collective-permute-start.3
  198.5 3.4 %collective-permute-done.3 = bf16[768,768]{1,0:T(8,128)(2,1)S(1)} collective-permute-done((bf16[768,768]{1,0:T(8,128)(2,1)S(1)}, bf16[768,768]{1,0:T(8,128)(2,1)S(1)}, u32[]{:S(2)}, u32[]{:S(2)}) %collective-permute-start.3) | collective-permute-done | bytes 1179680 | tf_op jit(solution)/shard_map/ppermute | solution.py:31
  202.0 0.3 fusion.35
  202.3 1.3 collective-permute-start.4
  203.6 16.8 %collective-permute-done.4 = bf16[768,768]{1,0:T(8,128)(2,1)S(1)} collective-permute-done((bf16[768,768]{1,0:T(8,128)(2,1)S(1)}, bf16[768,768]{1,0:T(8,128)(2,1)S(1)}, u32[]{:S(2)}, u32[]{:S(2)}) %collective-permute-start.4) | collective-permute-done | bytes 1179680 | tf_op jit(solution)/shard_map/ppermute | solution.py:33
  220.4 1.7 convert_add_fusion.3
  222.1 0.0 collective-permute-done
  222.1 0.0 collective-permute-done.1
  222.1 0.0 collective-permute-done.2
  222.1 4.8 %fusion.49 = (bf16[768,768]{1,0:T(8,128)(2,1)S(1)}, f32[768,768]{1,0:T(8,128)S(1)}) fusion(bf16[2048,768]{1,0:T(8,128)(2,1)S(1)} %fusion.12, bf16[2048,768]{1,0:T(8,128)(2,1)} %collective-permute-done.2, f32[768]{0:T(1024)S(1)} %get-tuple-element.22, f32[768]{0:T(1024)S(1)} %get-tuple-element.39), kind=kOutput, calls=%fused_computation.84 | convolution fusion | flops 2425946112 | bytes 9836544 | tf_op jit(solution)/shard_map/dot_general | solution.py:24
  226.9 1.5 collective-permute-start.5
  228.4 4.8 %fusion.48 = (bf16[768,768]{1,0:T(8,128)(2,1)S(1)}, f32[768,768]{1,0:T(8,128)S(1)}) fusion(bf16[2048,768]{1,0:T(8,128)(2,1)S(1)} %fusion.12, bf16[2048,768]{1,0:T(8,128)(2,1)} %collective-permute-done, f32[768]{0:T(1024)S(1)} %get-tuple-element.23, f32[768]{0:T(1024)S(1)} %get-tuple-element.37), kind=kOutput, calls=%fused_computation.83 | convolution fusion | flops 2425946112 | bytes 9836544 | tf_op jit(solution)/shard_map/dot_general | solution.py:24
  233.3 0.0 copy-start.1
  233.3 1.3 collective-permute-start.7
  234.6 4.8 %fusion.47 = (bf16[768,768]{1,0:T(8,128)(2,1)S(1)}, f32[768,768]{1,0:T(8,128)S(1)}) fusion(bf16[2048,768]{1,0:T(8,128)(2,1)S(1)} %fusion.12, bf16[2048,768]{1,0:T(8,128)(2,1)} %collective-permute-done.1, f32[768]{0:T(1024)S(1)} %get-tuple-element.25, f32[768]{0:T(1024)S(1)} %get-tuple-element.38), kind=kOutput, calls=%fused_computation.82 | convolution fusion | flops 2425946112 | bytes 9836544 | tf_op jit(solution)/shard_map/dot_general | solution.py:24
  239.4 0.0 copy-start.3
  239.4 3.2 %collective-permute-start.9 = (bf16[768,768]{1,0:T(8,128)(2,1)S(1)}, bf16[768,768]{1,0:T(8,128)(2,1)S(1)}, u32[]{:S(2)}, u32[]{:S(2)}) collective-permute-start(bf16[768,768]{1,0:T(8,128)(2,1)S(1)} %get-tuple-element.30), channel_id=1, source_target_pairs={{0,1},{2,3},{4,5},{6,7},{8,9},{10,11},{12,13},{14,15},{16,17},{18,... | collective-permute-start | bytes 3538952 | tf_op jit(solution)/shard_map/ppermute | solution.py:31
  242.6 0.0 collective-permute-done.5
  242.6 1.3 fusion.36
  243.9 1.7 collective-permute-start.6
  245.6 0.0 collective-permute-done.7
  245.6 0.0 copy-done.1
  245.6 1.4 fusion.37
  247.0 0.0 copy-done.6
  247.0 2.5 collective-permute-start.8
  249.5 0.0 collective-permute-done.9
  249.5 0.0 copy-done.3
  249.5 1.5 fusion.38
  251.0 0.0 copy-done.8
  251.0 1.8 collective-permute-start.10
  252.8 0.6 dynamic_slice.41
  254.0 0.0 collective-permute-done.6
  254.0 1.7 add_bitcast_fusion.2
  255.8 0.0 copy-start.4
  255.8 0.0 copy-start.9
  255.8 14.3 %collective-permute-done.8 = bf16[768,768]{1,0:T(8,128)(2,1)} collective-permute-done((bf16[768,768]{1,0:T(8,128)(2,1)}, bf16[768,768]{1,0:T(8,128)(2,1)}, u32[]{:S(2)}, u32[]{:S(2)}) %collective-permute-start.8) | collective-permute-done | bytes 1179680 | tf_op jit(solution)/shard_map/ppermute | solution.py:33
  270.1 0.0 copy-done.2
  270.1 1.7 add_bitcast_fusion.1
  271.8 0.0 collective-permute-done.10
  271.8 1.8 add_bitcast_fusion
  273.6 0.2 copy-done.5
  273.8 1.2 fusion.45
  275.1 0.7 collective-permute-start.11
  275.7 0.0 copy-done.11
  275.7 0.6 dynamic-slice.8
  277.0 0.0 collective-permute-done.11
  277.0 13.8 %all-reduce = f32[768]{0:T(1024)S(1)} all-reduce(f32[768]{0:T(1024)S(1)} %add.81), channel_id=2, replica_groups=mesh['var'=8,'samp'=4] {'samp'}, use_global_device_ids=true, to_apply=%region_6.7.clone | all-reduce | flops 768 | bytes 6144
  290.8 0.6 dynamic-slice_multiply_fusion
  (21 shorter events, 0.1 us)
Async XLA Ops:
  6.5 182.2 %all-gather.2.cloned.1.call-start = ((), (), s32[]{:S(2)}) async-start(), calls=%async_computation | async-start | bytes 2433024 | tf_op jit(solution)/shard_map/all_gather | solution.py:41
  6.5 6.3 %copy-start = (bf16[2048,768]{1,0:T(8,128)(2,1)S(1)}, bf16[2048,768]{1,0:T(8,128)(2,1)}, u32[]{:S(2)}) copy-start(bf16[2048,768]{1,0:T(8,128)(2,1)} %param.3) | copy-start | bytes 9437188
  12.2 0.6 copy-start.10
  18.1 204.0 %collective-permute-start = (bf16[2048,768]{1,0:T(8,128)(2,1)}, bf16[2048,768]{1,0:T(8,128)(2,1)}, u32[]{:S(2)}, u32[]{:S(2)}) collective-permute-start(bf16[2048,768]{1,0:T(8,128)(2,1)} %compare_select_fusion), channel_id=1, source_target_pairs={{8,0},{12,4},{16,8},{20,12},{24,16},{28,20},{9,1},{13,5},{17,9},{2... | collective-permute-start | bytes 9437192 | tf_op jit(solution)/shard_map/ppermute | solution.py:14
  19.4 202.7 %collective-permute-start.1 = (bf16[2048,768]{1,0:T(8,128)(2,1)}, bf16[2048,768]{1,0:T(8,128)(2,1)}, u32[]{:S(2)}, u32[]{:S(2)}) collective-permute-start(bf16[2048,768]{1,0:T(8,128)(2,1)} %compare_select_fusion), channel_id=1, source_target_pairs={{0,12},{4,16},{8,20},{12,24},{16,28},{1,13},{5,17},{9,21},{13,25},... | collective-permute-start | bytes 9437192 | tf_op jit(solution)/shard_map/ppermute | solution.py:14
  28.1 194.0 %collective-permute-start.2 = (bf16[2048,768]{1,0:T(8,128)(2,1)}, bf16[2048,768]{1,0:T(8,128)(2,1)}, u32[]{:S(2)}, u32[]{:S(2)}) collective-permute-start(bf16[2048,768]{1,0:T(8,128)(2,1)} %compare_select_fusion), channel_id=1, source_target_pairs={{4,0},{8,4},{12,8},{16,12},{20,16},{24,20},{28,24},{5,1},{9,5},{13... | collective-permute-start | bytes 9437192 | tf_op jit(solution)/shard_map/ppermute | solution.py:14
  197.2 4.7 %collective-permute-start.3 = (bf16[768,768]{1,0:T(8,128)(2,1)S(1)}, bf16[768,768]{1,0:T(8,128)(2,1)S(1)}, u32[]{:S(2)}, u32[]{:S(2)}) collective-permute-start(bf16[768,768]{1,0:T(8,128)(2,1)S(1)} %get-tuple-element.28), channel_id=1, source_target_pairs={{1,0},{3,2},{5,4},{7,6},{9,8},{11,10},{13,12},{15,14},{17,16},{19,... | collective-permute-start | bytes 3538952 | tf_op jit(solution)/shard_map/ppermute | solution.py:31
  202.3 18.1 %collective-permute-start.4 = (bf16[768,768]{1,0:T(8,128)(2,1)S(1)}, bf16[768,768]{1,0:T(8,128)(2,1)S(1)}, u32[]{:S(2)}, u32[]{:S(2)}) collective-permute-start(bf16[768,768]{1,0:T(8,128)(2,1)S(1)} %fusion.35), channel_id=1, source_target_pairs={{2,0},{6,4},{10,8},{14,12},{18,16},{22,20},{26,24},{30,28}} | collective-permute-start | bytes 3538952 | tf_op jit(solution)/shard_map/ppermute | solution.py:33
  226.9 15.7 %collective-permute-start.5 = (bf16[768,768]{1,0:T(8,128)(2,1)S(1)}, bf16[768,768]{1,0:T(8,128)(2,1)S(1)}, u32[]{:S(2)}, u32[]{:S(2)}) collective-permute-start(bf16[768,768]{1,0:T(8,128)(2,1)S(1)} %get-tuple-element.34), channel_id=1, source_target_pairs={{0,1},{2,3},{4,5},{6,7},{8,9},{10,11},{12,13},{14,15},{16,17},{18,... | collective-permute-start | bytes 3538952 | tf_op jit(solution)/shard_map/ppermute | solution.py:31
  233.3 12.3 %copy-start.1 = (f32[768,768]{1,0:T(8,128)}, f32[768,768]{1,0:T(8,128)S(1)}, u32[]{:S(2)}) copy-start(f32[768,768]{1,0:T(8,128)S(1)} %get-tuple-element.33) | copy-start | bytes 7077892
  233.3 12.3 %collective-permute-start.7 = (bf16[768,768]{1,0:T(8,128)(2,1)S(1)}, bf16[768,768]{1,0:T(8,128)(2,1)S(1)}, u32[]{:S(2)}, u32[]{:S(2)}) collective-permute-start(bf16[768,768]{1,0:T(8,128)(2,1)S(1)} %get-tuple-element.32), channel_id=1, source_target_pairs={{1,0},{3,2},{5,4},{7,6},{9,8},{11,10},{13,12},{15,14},{17,16},{19,... | collective-permute-start | bytes 3538952 | tf_op jit(solution)/shard_map/ppermute | solution.py:31
  239.4 10.1 %copy-start.3 = (f32[768,768]{1,0:T(8,128)}, f32[768,768]{1,0:T(8,128)S(1)}, u32[]{:S(2)}) copy-start(f32[768,768]{1,0:T(8,128)S(1)} %get-tuple-element.31) | copy-start | bytes 7077892
  239.4 10.1 %collective-permute-start.9 = (bf16[768,768]{1,0:T(8,128)(2,1)S(1)}, bf16[768,768]{1,0:T(8,128)(2,1)S(1)}, u32[]{:S(2)}, u32[]{:S(2)}) collective-permute-start(bf16[768,768]{1,0:T(8,128)(2,1)S(1)} %get-tuple-element.30), channel_id=1, source_target_pairs={{0,1},{2,3},{4,5},{6,7},{8,9},{10,11},{12,13},{14,15},{16,17},{18,... | collective-permute-start | bytes 3538952 | tf_op jit(solution)/shard_map/ppermute | solution.py:31
  243.9 10.1 %collective-permute-start.6 = (bf16[768,768]{1,0:T(8,128)(2,1)}, bf16[768,768]{1,0:T(8,128)(2,1)}, u32[]{:S(2)}, u32[]{:S(2)}) collective-permute-start(bf16[768,768]{1,0:T(8,128)(2,1)} %fusion.36), channel_id=1, source_target_pairs={{3,1},{7,5},{11,9},{15,13},{19,17},{23,21},{27,25},{31,29}} | collective-permute-start | bytes 3538952 | tf_op jit(solution)/shard_map/ppermute | solution.py:33
  245.6 1.4 copy-start.6
  247.0 23.1 %collective-permute-start.8 = (bf16[768,768]{1,0:T(8,128)(2,1)}, bf16[768,768]{1,0:T(8,128)(2,1)}, u32[]{:S(2)}, u32[]{:S(2)}) collective-permute-start(bf16[768,768]{1,0:T(8,128)(2,1)} %fusion.37), channel_id=1, source_target_pairs={{0,2},{4,6},{8,10},{12,14},{16,18},{20,22},{24,26},{28,30}} | collective-permute-start | bytes 3538952 | tf_op jit(solution)/shard_map/ppermute | solution.py:33
  249.5 1.5 copy-start.8
  249.5 3.3 %copy-start.12 = (s32[4]{0:T(128)S(1)}, s32[4]{0:T(128)}, u32[]{:S(2)}) copy-start(s32[4]{0:T(128)} %constant.83.clone) | copy-start | bytes 52
  251.0 20.8 %collective-permute-start.10 = (bf16[768,768]{1,0:T(8,128)(2,1)}, bf16[768,768]{1,0:T(8,128)(2,1)}, u32[]{:S(2)}, u32[]{:S(2)}) collective-permute-start(bf16[768,768]{1,0:T(8,128)(2,1)} %fusion.38), channel_id=1, source_target_pairs={{1,3},{5,7},{9,11},{13,15},{17,19},{21,23},{25,27},{29,31}} | collective-permute-start | bytes 3538952 | tf_op jit(solution)/shard_map/ppermute | solution.py:33
  254.0 16.1 %copy-start.2 = (f32[768,768]{1,0:T(8,128)S(1)}, f32[768,768]{1,0:T(8,128)}, u32[]{:S(2)}) copy-start(f32[768,768]{1,0:T(8,128)} %copy-done.1) | copy-start | bytes 7077892
  254.0 16.1 %copy-start.7 = (bf16[768,768]{1,0:T(8,128)(2,1)S(1)}, bf16[768,768]{1,0:T(8,128)(2,1)}, u32[]{:S(2)}) copy-start(bf16[768,768]{1,0:T(8,128)(2,1)} %copy-done.6) | copy-start | bytes 3538948
  255.8 16.0 %copy-start.4 = (f32[768,768]{1,0:T(8,128)S(1)}, f32[768,768]{1,0:T(8,128)}, u32[]{:S(2)}) copy-start(f32[768,768]{1,0:T(8,128)} %copy-done.3) | copy-start | bytes 7077892
  255.8 16.0 %copy-start.9 = (bf16[768,768]{1,0:T(8,128)(2,1)S(1)}, bf16[768,768]{1,0:T(8,128)(2,1)}, u32[]{:S(2)}) copy-start(bf16[768,768]{1,0:T(8,128)(2,1)} %copy-done.8) | copy-start | bytes 3538948
  271.8 2.0 copy-start.5
  273.8 1.9 copy-start.11
  275.1 1.9 collective-permute-start.11
Sparse Core Ops, SparseCore 0:
  12.9 175.7 all-gather.1
